TPU v7x, 32 devices: a whole 2x2x4 slice. The times are simulated.
32 devices in a mesh: tile: 4 (over x, core), mem: 8 (over z, y).
Axes of the slice: x: 2, y: 2, z: 4, core: 2. Of those that a mesh axis runs over, the one named last changes fastest.
Arguments:
- perturbations: bfloat16 [32, 2, 16, 16, 512], P('mem', None, 'tile'), may hold values from -3 to 3
- innovations: float32 [4, 32768], P('tile', 'mem'), may hold values from -6 to 6
- obs_weight: float32 [4, 32768], P('tile', 'mem'), may hold values from 0.4 to 4
- obs_cell: int32 [4, 32768], P('tile', 'mem'), may hold values from 0 to 8191
- row_start: int32 [16], P('tile'), may hold values from 0 to 511
- row_length: int32 [16], P('tile'), may hold values from 256 to 512
- lat_rate: float32 [16], replicated, may hold values from 0.3 to 0.4
- lon_rate: float32 [16], replicated, may hold values from 0.02 to 0.1
Outputs:
- control: float32 [32, 16, 16, 512], P('mem', 'tile')
- increment: float32 [2, 16, 8192], P(None, 'tile', 'mem')
All inputs are finite; a program needn't handle non-finite values.
Results may differ from a plain program's by a relative error of at most 0.0003.
Values sent between devices are 32-bit elements; how exact they have to be, the bound alone decides.
No kernel may reach another device: no remote copies, remote signals or barrier semaphores. Data moves between devices by JAX's collectives and lax.ppermute only.
A program may use at most 64 MiB of HBM per device.

v0:
```python
import jax
import jax.numpy as jnp
from jax import lax
from jax.sharding import PartitionSpec as P

ITERS = 2
STEPS = 8
DEPTH = 4


def with_halo(block, sides, width):
    for axis, dim in sides:
        count = lax.axis_size(axis)
        forward = [(i, i + 1) for i in range(count - 1)]
        backward = [(target, source) for source, target in forward]
        low = lax.ppermute(
            lax.slice_in_dim(block, block.shape[dim] - width, None, axis=dim), axis, forward
        )
        high = lax.ppermute(lax.slice_in_dim(block, 0, width, axis=dim), axis, backward)
        block = jnp.concatenate([low, block, high], axis=dim)
    return block


def row_mask(starts, lengths, nlon):
    lon = lax.broadcasted_iota(jnp.int32, (starts.shape[0], nlon), 1)
    rel = (lon - starts[:, None]) % nlon
    return jnp.where(rel < lengths[:, None], 1.0, 0.0).astype(jnp.float32)[:, None, :]


def diffuse_step(field, mask, lat_rate, lon_rate):
    zero = jnp.zeros_like(field[:, :1])
    north = jnp.concatenate([field[:, 1:], zero], axis=1)
    south = jnp.concatenate([zero, field[:, :-1]], axis=1)
    east = jnp.roll(field, -1, axis=3)
    west = jnp.roll(field, 1, axis=3)
    lat_term = north + south - 2.0 * field
    lon_term = east + west - 2.0 * field
    return mask * (field + lat_rate[:, None] * lat_term + lon_rate[:, None] * lon_term)


def global_sum(value):
    return lax.psum(value, ("tile", "mem"))


def body(
    perturbations, innovations, obs_weight, obs_cell, row_start, row_length, lat_rate, lon_rate
):
    slots = perturbations.shape[1]
    lat_rows = perturbations.shape[2]
    levels = perturbations.shape[3]
    nlon = perturbations.shape[4]
    groups = lax.axis_size("mem")
    cols = levels * nlon
    shard_cols = cols // groups
    own_mask = row_mask(row_start, row_length, nlon)
    tables = with_halo(jnp.stack([row_start, row_length]), (("tile", 1),), DEPTH)
    wide_mask = row_mask(tables[0], tables[1], nlon)

    def smooth(field):
        current = own_mask * field
        for block in range(STEPS // DEPTH):
            wide = with_halo(current, (("tile", 1),), DEPTH)
            for inner in range(DEPTH):
                wide = diffuse_step(wide, wide_mask, lat_rate, lon_rate)
            current = wide[:, DEPTH : DEPTH + lat_rows]
        return current

    def forward(control):
        smoothed = smooth(control)
        summed = jnp.sum(perturbations * smoothed[:, None], axis=0)
        return summed.reshape(slots, lat_rows, cols)

    def adjoint(gradient):
        field = gradient.reshape(slots, lat_rows, levels, nlon)
        return smooth(jnp.sum(perturbations * field[None], axis=1))

    local_cells = obs_cell[0]
    innov = innovations[0]
    weight = obs_weight[0]

    def grid_of(values):
        flat = jnp.zeros((slots * lat_rows * shard_cols,), jnp.float32).at[local_cells].add(values)
        gradient = flat.reshape(slots, lat_rows, shard_cols)
        gradient = lax.all_gather(gradient, "mem", axis=2, tiled=True)
        return gradient

    residual = adjoint(grid_of(weight * innov))
    direction = residual
    control = jnp.zeros_like(residual)
    increment = jnp.zeros((slots, lat_rows, shard_cols), jnp.float32)
    norm_now = global_sum(jnp.sum(residual * residual))
    for step in range(ITERS):
        local = forward(direction)
        state = lax.psum_scatter(local, "mem", scatter_dimension=2, tiled=True)
        image = direction + adjoint(grid_of(weight * state.reshape(-1)[local_cells]))
        alpha = norm_now / global_sum(jnp.sum(direction * image))
        control = control + alpha * direction
        increment = increment + alpha * state
        if step + 1 < ITERS:
            residual = residual - alpha * image
            norm_next = global_sum(jnp.sum(residual * residual))
            direction = residual + norm_next / norm_now * direction
            norm_now = norm_next
    return (control, increment)


def solution(mesh):
    return jax.shard_map(
        body,
        mesh=mesh,
        in_specs=(
            P("mem", None, "tile", None, None),
            P("tile", "mem"),
            P("tile", "mem"),
            P("tile", "mem"),
            P("tile"),
            P("tile"),
            P(),
            P(),
        ),
        out_specs=(P("mem", "tile", None, None), P(None, "tile", "mem")),
        check_vma=False,
    )
```

profile of v0, /device:TPU:0, one launch (start us, length us, event | category | flops | bytes accessed | tf_op | source)
XLA Modules:
  0.0 780.5 jit_solution(5411406026107221729)
XLA Ops:
  7.9 1.3 collective-permute-start.1
  9.2 3.0 collective-permute-start
  14.5 21.9 %scatter_custom_fusion = f32[8192]{0:T(1024)S(1)} fusion(s32[4096]{0:T(1024)S(1)} %bitcast.39, f32[4096]{0:T(1024)S(1)} %mul.402, f32[]{:T(128)} %constant.31.clone.1), kind=kCustom, calls=%fused_computation.314 | custom fusion | flops 4096 | bytes 32772 | tf_op jit(solution)/shard_map/scatter-add | solution.py:82
  36.4 32.6 %all_gather.9 = f32[2,4,8192]{2,1,0:T(4,128)S(1)} all-gather(f32[2,4,1024]{2,1,0:T(4,128)S(1)} %reshape.142), channel_id=1, replica_groups=mesh['tile'=4,'mem'=8] {'mem'}, dimensions={2}, use_global_device_ids=true | all-gather | bytes 294912 | tf_op jit(solution)/shard_map/all_gather | solution.py:84
  69.2 1.2 fusion.120
  70.4 1.3 collective-permute-start.3
  71.7 3.1 collective-permute-start.2
  75.1 1.2 collective-permute-done.2
  80.0 1.2 fusion.7
  82.4 1.2 fusion.11
  85.0 1.3 collective-permute-start.5
  86.3 8.6 %collective-permute-start.4 = (f32[4,4,16,512]{3,2,1,0:T(8,128)S(1)}, f32[4,4,16,512]{3,2,1,0:T(8,128)S(1)}, u32[]{:S(2)}, u32[]{:S(2)}) collective-permute-start(f32[4,4,16,512]{3,2,1,0:T(8,128)S(1)} %fusion.203), channel_id=1, source_target_pairs={{0,8},{8,16},{16,24},{1,9},{9,17},{17,25},{2,10},{10,18},{18,26},{... | collective-permute-start | bytes 1572872 | tf_op jit(solution)/shard_map/ppermute | solution.py:16
  94.9 1.2 collective-permute-done.4
  99.7 1.2 fusion.19
  102.1 1.2 fusion.23
  104.8 1.3 collective-permute-start.7
  106.1 10.2 %collective-permute-start.6 = (f32[4,4,16,512]{3,2,1,0:T(8,128)S(1)}, f32[4,4,16,512]{3,2,1,0:T(8,128)S(1)}, u32[]{:S(2)}, u32[]{:S(2)}) collective-permute-start(f32[4,4,16,512]{3,2,1,0:T(8,128)S(1)} %get-tuple-element.7), channel_id=1, source_target_pairs={{0,8},{8,16},{16,24},{1,9},{9,17},{17,25},{2,10},{10,18},{18,26},{... | collective-permute-start | bytes 1572872 | tf_op jit(solution)/shard_map/ppermute | solution.py:16
  120.9 1.2 fusion.31
  125.9 1.3 collective-permute-start.9
  127.2 9.8 %collective-permute-start.8 = (f32[4,4,16,512]{3,2,1,0:T(8,128)S(1)}, f32[4,4,16,512]{3,2,1,0:T(8,128)S(1)}, u32[]{:S(2)}, u32[]{:S(2)}) collective-permute-start(f32[4,4,16,512]{3,2,1,0:T(8,128)S(1)} %fusion.187), channel_id=1, source_target_pairs={{0,8},{8,16},{16,24},{1,9},{9,17},{17,25},{2,10},{10,18},{18,26},{... | collective-permute-start | bytes 1572872 | tf_op jit(solution)/shard_map/ppermute | solution.py:16
  137.1 1.3 collective-permute-done.8
  142.0 1.2 fusion.43
  147.8 5.9 copy.14
  153.7 8.8 %reshape.189 = f32[8192,8]{1,0:T(8,128)} reshape(f32[8192,2,4]{2,1,0:T(2,128)} %bitcast.28) | data formatting | bytes 524288
  162.7 96.8 %reduce-scatter.7.cloned.1.call-done = f32[1024,8]{1,0:T(8,128)} async-done(((f32[8192,8]{1,0:T(8,128)}), f32[1024,8]{1,0:T(8,128)}) %reduce-scatter.7.cloned.1.call-update) | async-done | bytes 32784
  259.5 1.6 reshape.190
  261.6 23.0 %gather_fusion = f32[4096]{0:T(1024)S(1)} fusion(f32[8192]{0:T(1024)S(1)} %bitcast.27, s32[4096]{0:T(1024)S(1)} %broadcast_clamp_fusion), kind=kCustom, calls=%fused_computation | custom fusion | bytes 49152 | tf_op jit(solution)/shard_map/gather | solution.py:95
  284.7 21.9 %scatter_custom_fusion.1 = f32[8192]{0:T(1024)S(1)} fusion(s32[4096]{0:T(1024)S(1)} %bitcast.41, f32[4096]{0:T(1024)S(1)} %mul.477, f32[]{:T(128)} %constant.31.clone.1), kind=kCustom, calls=%fused_computation.312 | custom fusion | flops 4096 | bytes 32772 | tf_op jit(solution)/shard_map/scatter-add | solution.py:82
  306.7 31.0 %all_gather.10 = f32[2,4,8192]{2,1,0:T(4,128)S(1)} all-gather(f32[2,4,1024]{2,1,0:T(4,128)S(1)} %reshape.145), channel_id=1, replica_groups=mesh['tile'=4,'mem'=8] {'mem'}, dimensions={2}, use_global_device_ids=true | all-gather | bytes 294912 | tf_op jit(solution)/shard_map/all_gather | solution.py:84
  338.0 1.3 collective-permute-start.11
  339.3 3.1 collective-permute-start.10
  342.4 1.5 collective-permute-done.10
  345.3 1.2 fusion.51
  347.5 1.2 fusion.55
  352.6 1.3 collective-permute-start.13
  353.9 8.7 %collective-permute-start.12 = (f32[4,4,16,512]{3,2,1,0:T(8,128)S(1)}, f32[4,4,16,512]{3,2,1,0:T(8,128)S(1)}, u32[]{:S(2)}, u32[]{:S(2)}) collective-permute-start(f32[4,4,16,512]{3,2,1,0:T(8,128)S(1)} %fusion.171), channel_id=1, source_target_pairs={{0,8},{8,16},{16,24},{1,9},{9,17},{17,25},{2,10},{10,18},{18,26},{... | collective-permute-start | bytes 1572872 | tf_op jit(solution)/shard_map/ppermute | solution.py:16
  367.3 1.2 fusion.67
  373.1 46.6 %all-reduce.80 = (f32[]{:T(128)}, f32[]{:T(128)}) all-reduce(f32[]{:T(128)} %get-tuple-element.3, f32[]{:T(128)} %get-tuple-element.2), channel_id=1, replica_groups=mesh['tile'=4,'mem'=8] {'tile','mem'}, use_global_device_ids=true, to_apply=%region_3.4 | all-reduce | flops 2 | bytes 16 | tf_op jit(solution)/shard_map/psum | solution.py:42
  421.7 41.2 %psum.30 = f32[]{:T(128)} all-reduce(f32[]{:T(128)} %multiply_reduce_fusion), channel_id=1, replica_groups=mesh['tile'=4,'mem'=8] {'tile','mem'}, use_global_device_ids=true, to_apply=%region_11.12 | all-reduce | flops 1 | bytes 8 | tf_op jit(solution)/shard_map/psum | solution.py:42
  464.3 1.3 collective-permute-start.15
  465.6 3.2 collective-permute-start.14
  468.8 1.3 collective-permute-done.14
  473.8 1.2 fusion.79
  478.8 1.3 collective-permute-start.17
  480.1 9.3 %collective-permute-start.16 = (f32[4,4,16,512]{3,2,1,0:T(8,128)S(1)}, f32[4,4,16,512]{3,2,1,0:T(8,128)S(1)}, u32[]{:S(2)}, u32[]{:S(2)}) collective-permute-start(f32[4,4,16,512]{3,2,1,0:T(8,128)S(1)} %fusion.154), channel_id=1, source_target_pairs={{0,8},{8,16},{16,24},{1,9},{9,17},{17,25},{2,10},{10,18},{18,26},{... | collective-permute-start | bytes 1572872 | tf_op jit(solution)/shard_map/ppermute | solution.py:16
  489.4 1.3 collective-permute-done.16
  494.4 1.2 fusion.91
  499.5 5.9 copy.15
  505.4 8.8 %reshape.191 = f32[8192,8]{1,0:T(8,128)} reshape(f32[8192,2,4]{2,1,0:T(2,128)} %bitcast.29) | data formatting | bytes 524288
  514.3 95.9 %reduce-scatter.9.cloned.1.call-done = f32[1024,8]{1,0:T(8,128)} async-done(((f32[8192,8]{1,0:T(8,128)}), f32[1024,8]{1,0:T(8,128)}) %reduce-scatter.9.cloned.1.call-update) | async-done | bytes 32784
  610.2 1.6 reshape.192
  612.4 23.0 %gather_fusion.1 = f32[4096]{0:T(1024)S(1)} fusion(f32[8192]{0:T(1024)S(1)} %bitcast.26, s32[4096]{0:T(1024)S(1)} %broadcast_clamp_fusion), kind=kCustom, calls=%fused_computation.1 | custom fusion | bytes 49152 | tf_op jit(solution)/shard_map/gather | solution.py:95
  635.4 21.9 %scatter_custom_fusion.2 = f32[8192]{0:T(1024)S(1)} fusion(s32[4096]{0:T(1024)S(1)} %bitcast.42, f32[4096]{0:T(1024)S(1)} %mul.556, f32[]{:T(128)} %constant.31.clone.1), kind=kCustom, calls=%fused_computation.310 | custom fusion | flops 4096 | bytes 32772 | tf_op jit(solution)/shard_map/scatter-add | solution.py:82
  657.4 31.1 %all_gather.11 = f32[2,4,8192]{2,1,0:T(4,128)S(1)} all-gather(f32[2,4,1024]{2,1,0:T(4,128)S(1)} %reshape.148), channel_id=1, replica_groups=mesh['tile'=4,'mem'=8] {'mem'}, dimensions={2}, use_global_device_ids=true | all-gather | bytes 294912 | tf_op jit(solution)/shard_map/all_gather | solution.py:84
  688.9 1.3 collective-permute-start.19
  690.2 3.1 collective-permute-start.18
  693.3 1.5 collective-permute-done.18
  698.4 1.2 fusion.103
  703.5 1.3 collective-permute-start.21
  704.8 8.4 %collective-permute-start.20 = (f32[4,4,16,512]{3,2,1,0:T(8,128)S(1)}, f32[4,4,16,512]{3,2,1,0:T(8,128)S(1)}, u32[]{:S(2)}, u32[]{:S(2)}) collective-permute-start(f32[4,4,16,512]{3,2,1,0:T(8,128)S(1)} %fusion.138), channel_id=1, source_target_pairs={{0,8},{8,16},{16,24},{1,9},{9,17},{17,25},{2,10},{10,18},{18,26},{... | collective-permute-start | bytes 1572872 | tf_op jit(solution)/shard_map/ppermute | solution.py:16
  713.2 1.3 collective-permute-done.20
  718.2 1.2 fusion.115
  722.8 1.2 fusion.125
  724.0 46.6 %psum.31 = f32[]{:T(128)} all-reduce(f32[]{:T(128)} %fusion.125), channel_id=1, replica_groups=mesh['tile'=4,'mem'=8] {'tile','mem'}, use_global_device_ids=true, to_apply=%region_17.18 | all-reduce | flops 1 | bytes 8 | tf_op jit(solution)/shard_map/psum | solution.py:42
  (222 shorter events, 81.7 us)
Async XLA Ops:
  7.2 252.3 %reduce-scatter.7.cloned.1.call-start = ((), (), s32[]{:S(2)}) async-start(), calls=%async_computation.2 | async-start | bytes 4718592
  7.9 66.9 %collective-permute-start.1 = (s32[2,4]{1,0:T(2,128)S(1)}, s32[2,4]{1,0:T(2,128)S(1)}, u32[]{:S(2)}, u32[]{:S(2)}) collective-permute-start(s32[2,4]{1,0:T(2,128)S(1)} %pad_add_fusion.10), channel_id=1, source_target_pairs={{8,0},{16,8},{24,16},{9,1},{17,9},{25,17},{10,2},{18,10},{26,18},{... | collective-permute-start | bytes 104 | tf_op jit(solution)/shard_map/ppermute | solution.py:19
  9.2 65.7 %collective-permute-start = (s32[2,4]{1,0:T(2,128)S(1)}, s32[2,4]{1,0:T(2,128)S(1)}, u32[]{:S(2)}, u32[]{:S(2)}) collective-permute-start(s32[2,4]{1,0:T(2,128)S(1)} %pad_add_fusion.10), channel_id=1, source_target_pairs={{0,8},{8,16},{16,24},{1,9},{9,17},{17,25},{2,10},{10,18},{18,26},{... | collective-permute-start | bytes 104 | tf_op jit(solution)/shard_map/ppermute | solution.py:16
  36.4 38.4 %copy-start.6 = (s32[4]{0:T(128)S(1)}, s32[4]{0:T(128)}, u32[]{:S(2)}) copy-start(s32[4]{0:T(128)} %param.13) | copy-start | bytes 52
  36.4 38.4 %copy-start.7 = (s32[4]{0:T(128)S(1)}, s32[4]{0:T(128)}, u32[]{:S(2)}) copy-start(s32[4]{0:T(128)} %param.12) | copy-start | bytes 52
  70.4 4.6 collective-permute-start.3
  71.7 4.6 collective-permute-start.2
  77.1 0.7 copy-start.1
  77.1 0.7 copy-start.2
  85.0 9.9 %collective-permute-start.5 = (f32[4,4,16,512]{3,2,1,0:T(8,128)S(1)}, f32[4,4,16,512]{3,2,1,0:T(8,128)S(1)}, u32[]{:S(2)}, u32[]{:S(2)}) collective-permute-start(f32[4,4,16,512]{3,2,1,0:T(8,128)S(1)} %fusion.203), channel_id=1, source_target_pairs={{8,0},{16,8},{24,16},{9,1},{17,9},{25,17},{10,2},{18,10},{26,18},{... | collective-permute-start | bytes 1572872 | tf_op jit(solution)/shard_map/ppermute | solution.py:19
  86.3 9.8 %collective-permute-start.4 = (f32[4,4,16,512]{3,2,1,0:T(8,128)S(1)}, f32[4,4,16,512]{3,2,1,0:T(8,128)S(1)}, u32[]{:S(2)}, u32[]{:S(2)}) collective-permute-start(f32[4,4,16,512]{3,2,1,0:T(8,128)S(1)} %fusion.203), channel_id=1, source_target_pairs={{0,8},{8,16},{16,24},{1,9},{9,17},{17,25},{2,10},{10,18},{18,26},{... | collective-permute-start | bytes 1572872 | tf_op jit(solution)/shard_map/ppermute | solution.py:16
  104.8 11.5 %collective-permute-start.7 = (f32[4,4,16,512]{3,2,1,0:T(8,128)S(1)}, f32[4,4,16,512]{3,2,1,0:T(8,128)S(1)}, u32[]{:S(2)}, u32[]{:S(2)}) collective-permute-start(f32[4,4,16,512]{3,2,1,0:T(8,128)S(1)} %get-tuple-element.7), channel_id=1, source_target_pairs={{8,0},{16,8},{24,16},{9,1},{17,9},{25,17},{10,2},{18,10},{26,18},{... | collective-permute-start | bytes 1572872 | tf_op jit(solution)/shard_map/ppermute | solution.py:19
  106.1 11.1 %collective-permute-start.6 = (f32[4,4,16,512]{3,2,1,0:T(8,128)S(1)}, f32[4,4,16,512]{3,2,1,0:T(8,128)S(1)}, u32[]{:S(2)}, u32[]{:S(2)}) collective-permute-start(f32[4,4,16,512]{3,2,1,0:T(8,128)S(1)} %get-tuple-element.7), channel_id=1, source_target_pairs={{0,8},{8,16},{16,24},{1,9},{9,17},{17,25},{2,10},{10,18},{18,26},{... | collective-permute-start | bytes 1572872 | tf_op jit(solution)/shard_map/ppermute | solution.py:16
  125.9 11.1 %collective-permute-start.9 = (f32[4,4,16,512]{3,2,1,0:T(8,128)S(1)}, f32[4,4,16,512]{3,2,1,0:T(8,128)S(1)}, u32[]{:S(2)}, u32[]{:S(2)}) collective-permute-start(f32[4,4,16,512]{3,2,1,0:T(8,128)S(1)} %fusion.187), channel_id=1, source_target_pairs={{8,0},{16,8},{24,16},{9,1},{17,9},{25,17},{10,2},{18,10},{26,18},{... | collective-permute-start | bytes 1572872 | tf_op jit(solution)/shard_map/ppermute | solution.py:19
  127.2 11.1 %collective-permute-start.8 = (f32[4,4,16,512]{3,2,1,0:T(8,128)S(1)}, f32[4,4,16,512]{3,2,1,0:T(8,128)S(1)}, u32[]{:S(2)}, u32[]{:S(2)}) collective-permute-start(f32[4,4,16,512]{3,2,1,0:T(8,128)S(1)} %fusion.187), channel_id=1, source_target_pairs={{0,8},{8,16},{16,24},{1,9},{9,17},{17,25},{2,10},{10,18},{18,26},{... | collective-permute-start | bytes 1572872 | tf_op jit(solution)/shard_map/ppermute | solution.py:16
  146.7 1.0 copy-start
  162.6 447.6 %reduce-scatter.9.cloned.1.call-start = ((), (), s32[]{:S(2)}) async-start(), calls=%async_computation.3 | async-start | bytes 4718592
  261.6 23.1 %copy-start.3 = (f32[2,4,1024]{2,1,0:T(4,128)}, f32[2,4,1024]{2,1,0:T(4,128)S(1)}, u32[]{:S(2)}) copy-start(f32[2,4,1024]{2,1,0:T(4,128)S(1)} %copy.11) | copy-start | bytes 98308
  261.6 23.1 %copy-start.5 = (f32[1,4096]{1,0:T(1,128)S(1)}, f32[1,4096]{1,0:T(1,128)}, u32[]{:S(2)}) copy-start(f32[1,4096]{1,0:T(1,128)} %param.10) | copy-start | bytes 49156
  338.0 4.4 collective-permute-start.11
  339.3 4.6 collective-permute-start.10
  352.6 10.0 %collective-permute-start.13 = (f32[4,4,16,512]{3,2,1,0:T(8,128)S(1)}, f32[4,4,16,512]{3,2,1,0:T(8,128)S(1)}, u32[]{:S(2)}, u32[]{:S(2)}) collective-permute-start(f32[4,4,16,512]{3,2,1,0:T(8,128)S(1)} %fusion.171), channel_id=1, source_target_pairs={{8,0},{16,8},{24,16},{9,1},{17,9},{25,17},{10,2},{18,10},{26,18},{... | collective-permute-start | bytes 1572872 | tf_op jit(solution)/shard_map/ppermute | solution.py:19
  353.9 9.8 %collective-permute-start.12 = (f32[4,4,16,512]{3,2,1,0:T(8,128)S(1)}, f32[4,4,16,512]{3,2,1,0:T(8,128)S(1)}, u32[]{:S(2)}, u32[]{:S(2)}) collective-permute-start(f32[4,4,16,512]{3,2,1,0:T(8,128)S(1)} %fusion.171), channel_id=1, source_target_pairs={{0,8},{8,16},{16,24},{1,9},{9,17},{17,25},{2,10},{10,18},{18,26},{... | collective-permute-start | bytes 1572872 | tf_op jit(solution)/shard_map/ppermute | solution.py:16
  464.3 4.5 collective-permute-start.15
  465.6 4.6 collective-permute-start.14
  478.8 10.6 %collective-permute-start.17 = (f32[4,4,16,512]{3,2,1,0:T(8,128)S(1)}, f32[4,4,16,512]{3,2,1,0:T(8,128)S(1)}, u32[]{:S(2)}, u32[]{:S(2)}) collective-permute-start(f32[4,4,16,512]{3,2,1,0:T(8,128)S(1)} %fusion.154), channel_id=1, source_target_pairs={{8,0},{16,8},{24,16},{9,1},{17,9},{25,17},{10,2},{18,10},{26,18},{... | collective-permute-start | bytes 1572872 | tf_op jit(solution)/shard_map/ppermute | solution.py:19
  480.1 10.5 %collective-permute-start.16 = (f32[4,4,16,512]{3,2,1,0:T(8,128)S(1)}, f32[4,4,16,512]{3,2,1,0:T(8,128)S(1)}, u32[]{:S(2)}, u32[]{:S(2)}) collective-permute-start(f32[4,4,16,512]{3,2,1,0:T(8,128)S(1)} %fusion.154), channel_id=1, source_target_pairs={{0,8},{8,16},{16,24},{1,9},{9,17},{17,25},{2,10},{10,18},{18,26},{... | collective-permute-start | bytes 1572872 | tf_op jit(solution)/shard_map/ppermute | solution.py:16
  688.9 4.4 collective-permute-start.19
  690.2 4.6 collective-permute-start.18
  703.5 9.7 %collective-permute-start.21 = (f32[4,4,16,512]{3,2,1,0:T(8,128)S(1)}, f32[4,4,16,512]{3,2,1,0:T(8,128)S(1)}, u32[]{:S(2)}, u32[]{:S(2)}) collective-permute-start(f32[4,4,16,512]{3,2,1,0:T(8,128)S(1)} %fusion.138), channel_id=1, source_target_pairs={{8,0},{16,8},{24,16},{9,1},{17,9},{25,17},{10,2},{18,10},{26,18},{... | collective-permute-start | bytes 1572872 | tf_op jit(solution)/shard_map/ppermute | solution.py:19
  704.8 9.7 %collective-permute-start.20 = (f32[4,4,16,512]{3,2,1,0:T(8,128)S(1)}, f32[4,4,16,512]{3,2,1,0:T(8,128)S(1)}, u32[]{:S(2)}, u32[]{:S(2)}) collective-permute-start(f32[4,4,16,512]{3,2,1,0:T(8,128)S(1)} %fusion.138), channel_id=1, source_target_pairs={{0,8},{8,16},{16,24},{1,9},{9,17},{17,25},{2,10},{10,18},{18,26},{... | collective-permute-start | bytes 1572872 | tf_op jit(solution)/shard_map/ppermute | solution.py:16
  724.0 48.9 %copy-start.4 = (f32[2,4,1024]{2,1,0:T(4,128)S(1)}, f32[2,4,1024]{2,1,0:T(4,128)}, u32[]{:S(2)}) copy-start(f32[2,4,1024]{2,1,0:T(4,128)} %copy-done.3) | copy-start | bytes 98308
Sparse Core Ops, SparseCore 0:
  162.7 96.7 reduce-scatter.6
  514.4 95.7 reduce-scatter.8
where the time goes:
time: 790 us; the launch traced here: 781 us
  blocking collectives  229 us (29%)
  waiting for transfers between devices  205 us (26%)
  local copies, waits for them, and re-layouts  126 us (16%)
  other arithmetic  115 us (15%)
  starting transfers between devices  84.6 us (11%)
  between operations  19.8 us (3%)
    unnamed x4, waiting for transfers between devices  193 us
    psum x3, blocking collectives, global_sum(): return lax.psum(value, ('tile', 'mem'))  134 us
    all_gather x3, blocking collectives, grid_of(): gradient = lax.all_gather(gradient, 'mem', axis=2, tiled=True)  94.7 us
    ppermute x11, starting transfers between devices, with_halo(): lax.ppermute(lax.slice_in_dim(block, block.shape[dim] - width, None, axis...  70.3 us
    scatter-add x3, other arithmetic, grid_of(): jnp.zeros((slots * lat_rows * shard_cols,), jnp.float32).at[local_cells]  65.8 us
    gather x2, local copies, waits for them, and re-layouts, body(): state.reshape(-1)[local_cells]  46.1 us
    mul x37, other arithmetic, diffuse_step(): mask * (field + lat_rate[:, None] * lat_term + lon_rate[:, None] * lon_term)  37.6 us
    unnamed x26, local copies, waits for them, and re-layouts  34.5 us
  transfers between devices with their start and end apart: 24, of which 12 were waited for; matrix products, arithmetic and copies ran while one was open for 3% of the time, Pallas kernels for 0%

commit v1 on v0

--- a/solution.py
+++ b/solution.py
@@ -35,7 +35,9 @@
     west = jnp.roll(field, 1, axis=3)
     lat_term = north + south - 2.0 * field
     lon_term = east + west - 2.0 * field
-    return mask * (field + lat_rate[:, None] * lat_term + lon_rate[:, None] * lon_term)
+    return mask * (
+        field + lat_rate[:, None, None, None] * lat_term + lon_rate[:, None, None, None] * lon_term
+    )
 
 
 def global_sum(value):
@@ -50,8 +52,20 @@
     levels = perturbations.shape[3]
     nlon = perturbations.shape[4]
     groups = lax.axis_size("mem")
-    cols = levels * nlon
-    shard_cols = cols // groups
+    own_levels = levels // groups
+    shard_cols = own_levels * nlon
+    first = lax.axis_index("mem") * own_levels
+    lat_own = lax.dynamic_slice_in_dim(lat_rate, first, own_levels)
+    lon_own = lax.dynamic_slice_in_dim(lon_rate, first, own_levels)
+
+    pert = lax.all_to_all(
+        perturbations.astype(jnp.float32).transpose(1, 3, 2, 0, 4),
+        "mem",
+        split_axis=1,
+        concat_axis=3,
+        tiled=True,
+    )
+
     own_mask = row_mask(row_start, row_length, nlon)
     tables = with_halo(jnp.stack([row_start, row_length]), (("tile", 1),), DEPTH)
     wide_mask = row_mask(tables[0], tables[1], nlon)
@@ -61,38 +75,37 @@
         for block in range(STEPS // DEPTH):
             wide = with_halo(current, (("tile", 1),), DEPTH)
             for inner in range(DEPTH):
-                wide = diffuse_step(wide, wide_mask, lat_rate, lon_rate)
+                wide = diffuse_step(wide, wide_mask, lat_own, lon_own)
             current = wide[:, DEPTH : DEPTH + lat_rows]
         return current
 
     def forward(control):
         smoothed = smooth(control)
-        summed = jnp.sum(perturbations * smoothed[:, None], axis=0)
-        return summed.reshape(slots, lat_rows, cols)
+        return jnp.sum(pert * smoothed[None], axis=3)
 
     def adjoint(gradient):
-        field = gradient.reshape(slots, lat_rows, levels, nlon)
-        return smooth(jnp.sum(perturbations * field[None], axis=1))
+        return smooth(jnp.sum(pert * gradient[:, :, :, None], axis=0))
 
     local_cells = obs_cell[0]
     innov = innovations[0]
     weight = obs_weight[0]
+    size = slots * lat_rows * shard_cols
+    state_shape = (slots, own_levels, lat_rows, nlon)
+    gathered = jnp.zeros((size, 2), jnp.float32).at[local_cells].add(
+        jnp.stack([weight * innov, weight], axis=1)
+    )
+    gathered = gathered.reshape(slots, lat_rows, own_levels, nlon, 2).transpose(4, 0, 2, 1, 3)
+    first_grad = gathered[0]
+    obs_diag = gathered[1]
 
-    def grid_of(values):
-        flat = jnp.zeros((slots * lat_rows * shard_cols,), jnp.float32).at[local_cells].add(values)
-        gradient = flat.reshape(slots, lat_rows, shard_cols)
-        gradient = lax.all_gather(gradient, "mem", axis=2, tiled=True)
-        return gradient
-
-    residual = adjoint(grid_of(weight * innov))
+    residual = adjoint(first_grad)
     direction = residual
     control = jnp.zeros_like(residual)
-    increment = jnp.zeros((slots, lat_rows, shard_cols), jnp.float32)
+    increment = jnp.zeros(state_shape, jnp.float32)
     norm_now = global_sum(jnp.sum(residual * residual))
     for step in range(ITERS):
-        local = forward(direction)
-        state = lax.psum_scatter(local, "mem", scatter_dimension=2, tiled=True)
-        image = direction + adjoint(grid_of(weight * state.reshape(-1)[local_cells]))
+        state = forward(direction)
+        image = direction + adjoint(obs_diag * state)
         alpha = norm_now / global_sum(jnp.sum(direction * image))
         control = control + alpha * direction
         increment = increment + alpha * state
@@ -101,6 +114,9 @@
             norm_next = global_sum(jnp.sum(residual * residual))
             direction = residual + norm_next / norm_now * direction
             norm_now = norm_next
+    control = lax.all_to_all(control, "mem", split_axis=2, concat_axis=0, tiled=True)
+    control = control.transpose(2, 1, 0, 3)
+    increment = increment.transpose(0, 2, 1, 3).reshape(slots, lat_rows, shard_cols)
     return (control, increment)
 
 

time: 790 us -> 463 us (0.59)
  waiting for transfers between devices: 205 us -> 38.4 us
  blocking collectives: 229 us -> 132 us
  local copies, waits for them, and re-layouts: 126 us -> 71.9 us
  starting transfers between devices: 84.6 us -> 107 us
  between operations: 19.8 us -> 6.4 us
  other arithmetic: 115 us -> 103 us
    unnamed x4 -> x0, waiting for transfers between devices: 193 us -> none
    all_gather x3 -> x0, blocking collectives: 94.7 us -> none  [grid_of(): gradient = lax.all_gather(gradient, 'mem', axis=2, tiled=True)]
    gather x2 -> x0, local copies, waits for them, and re-layouts: 46.1 us -> none  [body(): state.reshape(-1)[local_cells]]
    scatter-add x3 -> x1, other arithmetic: 65.8 us -> 24.6 us  [body(): jnp.zeros((size, 2), jnp.float32).at[local_cells]]
    unnamed x26 -> x23, local copies, waits for them, and re-layouts: 34.5 us -> 1.16 us
    ppermute x11, waiting for transfers between devices: 0.03 us -> 26.1 us  [with_halo(): lax.ppermute(lax.slice_in_dim(block, 0, width, axis=dim), axis, backward)]
    mul x40, other arithmetic: 38.3 us -> 60.5 us  [the longest x37 60.4 us: diffuse_step(): mask * (field + lat_rate[:, None, None, None] * lat_term + lon_rate[:, No...]
    all_to_all x0 -> x2, starting transfers between devices: none -> 12.5 us  [the longest x1 6.79 us: body(): lax.all_to_all(perturbations.astype(jnp.float32).transpose(1, 3, 2, 0, 4)...]
  transfers between devices with their start and end apart: 24 -> 24, of which waited for: 12 -> 13; matrix products, arithmetic and copies ran while one was open for 3% -> 7% of each run, Pallas kernels for 0% -> 0%
where the time goes in v1:
time: 463 us; the launch traced here: 457 us
  blocking collectives  132 us (29%)
  starting transfers between devices  107 us (23%)
  other arithmetic  103 us (22%)
  local copies, waits for them, and re-layouts  71.9 us (16%)
  waiting for transfers between devices  38.4 us (8%)
  between operations  6.4 us (1%)
    psum x3, blocking collectives, global_sum(): return lax.psum(value, ('tile', 'mem'))  132 us
    ppermute x11, starting transfers between devices, with_halo(): lax.ppermute(lax.slice_in_dim(block, block.shape[dim] - width, None, axis...  77.7 us
    mul x37, other arithmetic, diffuse_step(): mask * (field + lat_rate[:, None, None, None] * lat_term + lon_rate[:, No...  60.4 us
    slice x76, local copies, waits for them, and re-layouts, diffuse_step(): west = jnp.roll(field, 1, axis=3)  39 us
    ppermute x11, waiting for transfers between devices, with_halo(): lax.ppermute(lax.slice_in_dim(block, 0, width, axis=dim), axis, backward)  26.1 us
    scatter-add x1, other arithmetic, body(): jnp.zeros((size, 2), jnp.float32).at[local_cells]  24.6 us
    slice x40, local copies, waits for them, and re-layouts, diffuse_step(): north = jnp.concatenate([field[:, 1:], zero], axis=1)  20.6 us
    ppermute x11, starting transfers between devices, with_halo(): lax.ppermute(lax.slice_in_dim(block, 0, width, axis=dim), axis, backward)  16.5 us
  transfers between devices with their start and end apart: 24, of which 13 were waited for; matrix products, arithmetic and copies ran while one was open for 7% of the time, Pallas kernels for 0%

profile of v1, /device:TPU:0, one launch (start us, length us, event | category | flops | bytes accessed | tf_op | source)
XLA Modules:
  0.0 457.4 jit_solution(11030801299519888910)
XLA Ops:
  1.3 2.3 collective-permute-start
  6.2 1.7 copy.51
  7.9 6.8 %all-to-all-start = ((f32[2,16,4,4,512]{4,2,0,3,1:T(4,128)}), f32[2,16,4,4,512]{4,2,0,3,1:T(4,128)S(1)}, u32[]{:S(2)}, u32[]{:S(2)}) async-start(f32[2,16,4,4,512]{4,2,0,3,1:T(4,128)} %copy.51), calls=%async_computation | async-start | bytes 2097152 | tf_op jit(solution)/shard_map/all_to_all | solution.py:61
  15.6 24.6 %scatter_custom_fusion = f32[8192,2]{1,0:T(8,128)} fusion(s32[4096]{0:T(1024)S(1)} %bitcast.107, f32[4096,2]{1,0:T(8,128)S(1)} %copy.53, f32[]{:T(128)} %constant.21.clone.1), kind=kCustom, calls=%fused_computation.161 | custom fusion | flops 8192 | bytes 65540 | tf_op jit(solution)/shard_map/scatter-add | solution.py:94
  40.2 2.9 copy.54
  44.8 4.1 collective-permute-start.2
  50.5 3.6 collective-permute-done.3
  56.1 1.9 fusion.3
  59.5 1.7 fusion.7
  62.8 1.7 fusion.11
  67.1 9.1 %collective-permute-start.4 = (f32[2,4,32,512]{3,1,2,0:T(4,128)S(1)}, f32[2,4,32,512]{3,1,2,0:T(4,128)S(1)}, u32[]{:S(2)}, u32[]{:S(2)}) collective-permute-start(f32[2,4,32,512]{3,1,2,0:T(4,128)S(1)} %fusion.205), channel_id=1, source_target_pairs={{0,8},{8,16},{16,24},{1,9},{9,17},{17,25},{2,10},{10,18},{18,26},{... | collective-permute-start | bytes 1572872 | tf_op jit(solution)/shard_map/ppermute | solution.py:16
  77.8 2.3 collective-permute-done.5
  82.0 1.9 fusion.15
  85.5 1.7 fusion.19
  88.8 1.7 fusion.23
  93.2 8.6 %collective-permute-start.6 = (f32[2,4,32,512]{3,1,2,0:T(4,128)S(1)}, f32[2,4,32,512]{3,1,2,0:T(4,128)S(1)}, u32[]{:S(2)}, u32[]{:S(2)}) collective-permute-start(f32[2,4,32,512]{3,1,2,0:T(4,128)S(1)} %get-tuple-element.15), channel_id=1, source_target_pairs={{0,8},{8,16},{16,24},{1,9},{9,17},{17,25},{2,10},{10,18},{18,26},{... | collective-permute-start | bytes 1572872 | tf_op jit(solution)/shard_map/ppermute | solution.py:16
  101.8 1.8 collective-permute-start.7
  103.6 2.0 collective-permute-done.7
  107.6 1.9 fusion.27
  111.0 1.7 fusion.31
  114.3 1.7 fusion.35
  118.6 8.6 %collective-permute-start.8 = (f32[2,4,32,512]{3,1,2,0:T(4,128)S(1)}, f32[2,4,32,512]{3,1,2,0:T(4,128)S(1)}, u32[]{:S(2)}, u32[]{:S(2)}) collective-permute-start(f32[2,4,32,512]{3,1,2,0:T(4,128)S(1)} %fusion.189), channel_id=1, source_target_pairs={{0,8},{8,16},{16,24},{1,9},{9,17},{17,25},{2,10},{10,18},{18,26},{... | collective-permute-start | bytes 1572872 | tf_op jit(solution)/shard_map/ppermute | solution.py:16
  128.7 2.3 collective-permute-done.9
  133.0 2.0 fusion.39
  136.6 1.7 fusion.43
  139.9 1.7 fusion.47
  147.1 8.6 %collective-permute-start.10 = (f32[2,4,32,512]{3,1,2,0:T(4,128)S(1)}, f32[2,4,32,512]{3,1,2,0:T(4,128)S(1)}, u32[]{:S(2)}, u32[]{:S(2)}) collective-permute-start(f32[2,4,32,512]{3,1,2,0:T(4,128)S(1)} %bitcast.81), channel_id=1, source_target_pairs={{0,8},{8,16},{16,24},{1,9},{9,17},{17,25},{2,10},{10,18},{18,26},{... | collective-permute-start | bytes 1572872 | tf_op jit(solution)/shard_map/ppermute | solution.py:16
  157.2 2.3 collective-permute-done.11
  161.5 1.9 fusion.51
  164.9 1.7 fusion.55
  168.2 1.7 fusion.59
  172.5 8.6 %collective-permute-start.12 = (f32[2,4,32,512]{3,1,2,0:T(4,128)S(1)}, f32[2,4,32,512]{3,1,2,0:T(4,128)S(1)}, u32[]{:S(2)}, u32[]{:S(2)}) collective-permute-start(f32[2,4,32,512]{3,1,2,0:T(4,128)S(1)} %fusion.173), channel_id=1, source_target_pairs={{0,8},{8,16},{16,24},{1,9},{9,17},{17,25},{2,10},{10,18},{18,26},{... | collective-permute-start | bytes 1572872 | tf_op jit(solution)/shard_map/ppermute | solution.py:16
  181.1 1.7 collective-permute-start.13
  182.8 2.1 collective-permute-done.13
  186.9 1.9 fusion.63
  190.3 1.7 fusion.67
  193.6 1.7 fusion.71
  196.8 2.0 multiply_reduce_fusion.1
  198.9 46.3 %all-reduce.80 = (f32[]{:T(128)}, f32[]{:T(128)}) all-reduce(f32[]{:T(128)} %get-tuple-element.11, f32[]{:T(128)} %get-tuple-element.10), channel_id=1, replica_groups=mesh['tile'=4,'mem'=8] {'tile','mem'}, use_global_device_ids=true, to_apply=%region_3.4 | all-reduce | flops 2 | bytes 16 | tf_op jit(solution)/shard_map/psum | solution.py:44
  247.4 40.5 %psum.30 = f32[]{:T(128)} all-reduce(f32[]{:T(128)} %multiply_reduce_fusion), channel_id=1, replica_groups=mesh['tile'=4,'mem'=8] {'tile','mem'}, use_global_device_ids=true, to_apply=%region_9.10 | all-reduce | flops 1 | bytes 8 | tf_op jit(solution)/shard_map/psum | solution.py:44
  292.2 4.8 %collective-permute-done.15 = f32[2,4,32,512]{3,1,2,0:T(4,128)S(1)} collective-permute-done((f32[2,4,32,512]{3,1,2,0:T(4,128)S(1)}, f32[2,4,32,512]{3,1,2,0:T(4,128)S(1)}, u32[]{:S(2)}, u32[]{:S(2)}) %collective-permute-start.15) | collective-permute-done | bytes 524320 | tf_op jit(solution)/shard_map/ppermute | solution.py:19
  299.0 1.9 fusion.75
  302.5 1.7 fusion.79
  305.7 1.7 fusion.83
  310.0 9.1 %collective-permute-start.16 = (f32[2,4,32,512]{3,1,2,0:T(4,128)S(1)}, f32[2,4,32,512]{3,1,2,0:T(4,128)S(1)}, u32[]{:S(2)}, u32[]{:S(2)}) collective-permute-start(f32[2,4,32,512]{3,1,2,0:T(4,128)S(1)} %fusion.156), channel_id=1, source_target_pairs={{0,8},{8,16},{16,24},{1,9},{9,17},{17,25},{2,10},{10,18},{18,26},{... | collective-permute-start | bytes 1572872 | tf_op jit(solution)/shard_map/ppermute | solution.py:16
  319.2 1.7 collective-permute-start.17
  320.9 2.1 collective-permute-done.17
  324.9 1.9 fusion.87
  328.4 1.7 fusion.91
  331.7 1.7 fusion.95
  338.8 8.6 %collective-permute-start.18 = (f32[2,4,32,512]{3,1,2,0:T(4,128)S(1)}, f32[2,4,32,512]{3,1,2,0:T(4,128)S(1)}, u32[]{:S(2)}, u32[]{:S(2)}) collective-permute-start(f32[2,4,32,512]{3,1,2,0:T(4,128)S(1)} %bitcast.85), channel_id=1, source_target_pairs={{0,8},{8,16},{16,24},{1,9},{9,17},{17,25},{2,10},{10,18},{18,26},{... | collective-permute-start | bytes 1572872 | tf_op jit(solution)/shard_map/ppermute | solution.py:16
  348.9 2.3 collective-permute-done.19
  353.2 1.9 fusion.99
  356.7 1.7 fusion.103
  359.9 1.7 fusion.107
  364.2 8.6 %collective-permute-start.20 = (f32[2,4,32,512]{3,1,2,0:T(4,128)S(1)}, f32[2,4,32,512]{3,1,2,0:T(4,128)S(1)}, u32[]{:S(2)}, u32[]{:S(2)}) collective-permute-start(f32[2,4,32,512]{3,1,2,0:T(4,128)S(1)} %fusion.140), channel_id=1, source_target_pairs={{0,8},{8,16},{16,24},{1,9},{9,17},{17,25},{2,10},{10,18},{18,26},{... | collective-permute-start | bytes 1572872 | tf_op jit(solution)/shard_map/ppermute | solution.py:16
  374.4 2.3 collective-permute-done.21
  378.6 1.9 fusion.111
  382.1 1.7 fusion.115
  385.3 1.7 fusion.119
  388.5 2.1 fusion.127
  390.5 44.7 %psum.31 = f32[]{:T(128)} all-reduce(f32[]{:T(128)} %fusion.127), channel_id=1, replica_groups=mesh['tile'=4,'mem'=8] {'tile','mem'}, use_global_device_ids=true, to_apply=%region_13.14 | all-reduce | flops 1 | bytes 8 | tf_op jit(solution)/shard_map/psum | solution.py:44
  437.5 5.7 %all-to-all-start.1 = ((f32[2,4,32,512]{3,1,0,2:T(4,128)}), f32[2,4,32,512]{3,1,0,2:T(4,128)S(1)}, u32[]{:S(2)}, u32[]{:S(2)}) async-start(f32[2,4,32,512]{3,1,0,2:T(4,128)} %copy.63), calls=%async_computation.1 | async-start | bytes 1048576 | tf_op jit(solution)/shard_map/all_to_all | solution.py:117
  443.9 11.9 %all-to-all-done.1 = f32[2,4,32,512]{3,1,0,2:T(4,128)S(1)} async-done(((f32[2,4,32,512]{3,1,0,2:T(4,128)}), f32[2,4,32,512]{3,1,0,2:T(4,128)S(1)}, u32[]{:S(2)}, u32[]{:S(2)}) %all-to-all-start.1) | async-done | bytes 524320 | tf_op jit(solution)/shard_map/all_to_all | solution.py:117
  (220 shorter events, 102.1 us)
Async XLA Ops:
  1.3 49.0 %collective-permute-start = (s32[2,4]{1,0:T(2,128)S(1)}, s32[2,4]{1,0:T(2,128)S(1)}, u32[]{:S(2)}, u32[]{:S(2)}) collective-permute-start(s32[2,4]{1,0:T(2,128)S(1)} %pad_add_fusion.10), channel_id=1, source_target_pairs={{0,8},{8,16},{16,24},{1,9},{9,17},{17,25},{2,10},{10,18},{18,26},{... | collective-permute-start | bytes 104 | tf_op jit(solution)/shard_map/ppermute | solution.py:16
  3.7 46.6 %collective-permute-start.1 = (s32[2,4]{1,0:T(2,128)S(1)}, s32[2,4]{1,0:T(2,128)S(1)}, u32[]{:S(2)}, u32[]{:S(2)}) collective-permute-start(s32[2,4]{1,0:T(2,128)S(1)} %pad_add_fusion.10), channel_id=1, source_target_pairs={{8,0},{16,8},{24,16},{9,1},{17,9},{25,17},{10,2},{18,10},{26,18},{... | collective-permute-start | bytes 104 | tf_op jit(solution)/shard_map/ppermute | solution.py:19
  6.1 8.5 %copy-start.2 = (f32[1,4096]{1,0:T(1,128)S(1)}, f32[1,4096]{1,0:T(1,128)}, u32[]{:S(2)}) copy-start(f32[1,4096]{1,0:T(1,128)} %param.10) | copy-start | bytes 49156
  6.1 8.5 %copy-start.3 = (f32[1,4096]{1,0:T(1,128)S(1)}, f32[1,4096]{1,0:T(1,128)}, u32[]{:S(2)}) copy-start(f32[1,4096]{1,0:T(1,128)} %param.9) | copy-start | bytes 49156
  6.2 8.5 %copy-start.7 = (f32[16]{0:T(128)S(1)}, f32[16]{0:T(128)}, u32[]{:S(2)}) copy-start(f32[16]{0:T(128)} %param.14) | copy-start | bytes 196
  6.2 8.6 %copy-start.8 = (f32[16]{0:T(128)S(1)}, f32[16]{0:T(128)}, u32[]{:S(2)}) copy-start(f32[16]{0:T(128)} %param.15) | copy-start | bytes 196
  7.9 7.7 %copy-start.4 = (s32[1,4096]{1,0:T(1,128)S(1)}, s32[1,4096]{1,0:T(1,128)}, u32[]{:S(2)}) copy-start(s32[1,4096]{1,0:T(1,128)} %param.11) | copy-start | bytes 49156
  7.9 35.3 %all-to-all-start = ((f32[2,16,4,4,512]{4,2,0,3,1:T(4,128)}), f32[2,16,4,4,512]{4,2,0,3,1:T(4,128)S(1)}, u32[]{:S(2)}, u32[]{:S(2)}) async-start(f32[2,16,4,4,512]{4,2,0,3,1:T(4,128)} %copy.51), calls=%async_computation | async-start | bytes 2097152 | tf_op jit(solution)/shard_map/all_to_all | solution.py:61
  40.2 2.9 copy-start.5
  40.2 2.9 copy-start.6
  44.8 5.8 %collective-permute-start.2 = (f32[2,4,32,512]{3,1,2,0:T(4,128)S(1)}, f32[2,4,32,512]{3,1,2,0:T(4,128)S(1)}, u32[]{:S(2)}, u32[]{:S(2)}) collective-permute-start(f32[2,4,32,512]{3,1,2,0:T(4,128)S(1)} %bitcast.77), channel_id=1, source_target_pairs={{0,8},{8,16},{16,24},{1,9},{9,17},{17,25},{2,10},{10,18},{18,26},{... | collective-permute-start | bytes 1572872 | tf_op jit(solution)/shard_map/ppermute | solution.py:16
  48.8 5.3 %collective-permute-start.3 = (f32[2,4,32,512]{3,1,2,0:T(4,128)S(1)}, f32[2,4,32,512]{3,1,2,0:T(4,128)S(1)}, u32[]{:S(2)}, u32[]{:S(2)}) collective-permute-start(f32[2,4,32,512]{3,1,2,0:T(4,128)S(1)} %bitcast.78), channel_id=1, source_target_pairs={{8,0},{16,8},{24,16},{9,1},{17,9},{25,17},{10,2},{18,10},{26,18},{... | collective-permute-start | bytes 1572872 | tf_op jit(solution)/shard_map/ppermute | solution.py:19
  67.1 10.7 %collective-permute-start.4 = (f32[2,4,32,512]{3,1,2,0:T(4,128)S(1)}, f32[2,4,32,512]{3,1,2,0:T(4,128)S(1)}, u32[]{:S(2)}, u32[]{:S(2)}) collective-permute-start(f32[2,4,32,512]{3,1,2,0:T(4,128)S(1)} %fusion.205), channel_id=1, source_target_pairs={{0,8},{8,16},{16,24},{1,9},{9,17},{17,25},{2,10},{10,18},{18,26},{... | collective-permute-start | bytes 1572872 | tf_op jit(solution)/shard_map/ppermute | solution.py:16
  76.3 3.8 collective-permute-start.5
  93.2 10.4 %collective-permute-start.6 = (f32[2,4,32,512]{3,1,2,0:T(4,128)S(1)}, f32[2,4,32,512]{3,1,2,0:T(4,128)S(1)}, u32[]{:S(2)}, u32[]{:S(2)}) collective-permute-start(f32[2,4,32,512]{3,1,2,0:T(4,128)S(1)} %get-tuple-element.15), channel_id=1, source_target_pairs={{0,8},{8,16},{16,24},{1,9},{9,17},{17,25},{2,10},{10,18},{18,26},{... | collective-permute-start | bytes 1572872 | tf_op jit(solution)/shard_map/ppermute | solution.py:16
  101.8 3.8 collective-permute-start.7
  118.6 10.1 %collective-permute-start.8 = (f32[2,4,32,512]{3,1,2,0:T(4,128)S(1)}, f32[2,4,32,512]{3,1,2,0:T(4,128)S(1)}, u32[]{:S(2)}, u32[]{:S(2)}) collective-permute-start(f32[2,4,32,512]{3,1,2,0:T(4,128)S(1)} %fusion.189), channel_id=1, source_target_pairs={{0,8},{8,16},{16,24},{1,9},{9,17},{17,25},{2,10},{10,18},{18,26},{... | collective-permute-start | bytes 1572872 | tf_op jit(solution)/shard_map/ppermute | solution.py:16
  127.2 3.8 collective-permute-start.9
  145.4 14.4 %copy-start = (f32[2,2,4,512]{3,1,2,0:T(2,128)}, f32[2,2,4,512]{3,1,2,0:T(2,128)S(1)}, u32[]{:S(2)}) copy-start(f32[2,2,4,512]{3,1,2,0:T(2,128)S(1)} %fusion.123) | copy-start | bytes 98308
  147.1 10.1 %collective-permute-start.10 = (f32[2,4,32,512]{3,1,2,0:T(4,128)S(1)}, f32[2,4,32,512]{3,1,2,0:T(4,128)S(1)}, u32[]{:S(2)}, u32[]{:S(2)}) collective-permute-start(f32[2,4,32,512]{3,1,2,0:T(4,128)S(1)} %bitcast.81), channel_id=1, source_target_pairs={{0,8},{8,16},{16,24},{1,9},{9,17},{17,25},{2,10},{10,18},{18,26},{... | collective-permute-start | bytes 1572872 | tf_op jit(solution)/shard_map/ppermute | solution.py:16
  155.7 3.8 collective-permute-start.11
  172.5 10.3 %collective-permute-start.12 = (f32[2,4,32,512]{3,1,2,0:T(4,128)S(1)}, f32[2,4,32,512]{3,1,2,0:T(4,128)S(1)}, u32[]{:S(2)}, u32[]{:S(2)}) collective-permute-start(f32[2,4,32,512]{3,1,2,0:T(4,128)S(1)} %fusion.173), channel_id=1, source_target_pairs={{0,8},{8,16},{16,24},{1,9},{9,17},{17,25},{2,10},{10,18},{18,26},{... | collective-permute-start | bytes 1572872 | tf_op jit(solution)/shard_map/ppermute | solution.py:16
  181.1 3.8 collective-permute-start.13
  289.4 2.8 collective-permute-start.14
  290.7 6.3 %collective-permute-start.15 = (f32[2,4,32,512]{3,1,2,0:T(4,128)S(1)}, f32[2,4,32,512]{3,1,2,0:T(4,128)S(1)}, u32[]{:S(2)}, u32[]{:S(2)}) collective-permute-start(f32[2,4,32,512]{3,1,2,0:T(4,128)S(1)} %bitcast.90), channel_id=1, source_target_pairs={{8,0},{16,8},{24,16},{9,1},{17,9},{25,17},{10,2},{18,10},{26,18},{... | collective-permute-start | bytes 1572872 | tf_op jit(solution)/shard_map/ppermute | solution.py:19
  310.0 10.8 %collective-permute-start.16 = (f32[2,4,32,512]{3,1,2,0:T(4,128)S(1)}, f32[2,4,32,512]{3,1,2,0:T(4,128)S(1)}, u32[]{:S(2)}, u32[]{:S(2)}) collective-permute-start(f32[2,4,32,512]{3,1,2,0:T(4,128)S(1)} %fusion.156), channel_id=1, source_target_pairs={{0,8},{8,16},{16,24},{1,9},{9,17},{17,25},{2,10},{10,18},{18,26},{... | collective-permute-start | bytes 1572872 | tf_op jit(solution)/shard_map/ppermute | solution.py:16
  319.2 3.8 collective-permute-start.17
  338.8 10.1 %collective-permute-start.18 = (f32[2,4,32,512]{3,1,2,0:T(4,128)S(1)}, f32[2,4,32,512]{3,1,2,0:T(4,128)S(1)}, u32[]{:S(2)}, u32[]{:S(2)}) collective-permute-start(f32[2,4,32,512]{3,1,2,0:T(4,128)S(1)} %bitcast.85), channel_id=1, source_target_pairs={{0,8},{8,16},{16,24},{1,9},{9,17},{17,25},{2,10},{10,18},{18,26},{... | collective-permute-start | bytes 1572872 | tf_op jit(solution)/shard_map/ppermute | solution.py:16
  347.4 3.8 collective-permute-start.19
  364.2 10.1 %collective-permute-start.20 = (f32[2,4,32,512]{3,1,2,0:T(4,128)S(1)}, f32[2,4,32,512]{3,1,2,0:T(4,128)S(1)}, u32[]{:S(2)}, u32[]{:S(2)}) collective-permute-start(f32[2,4,32,512]{3,1,2,0:T(4,128)S(1)} %fusion.140), channel_id=1, source_target_pairs={{0,8},{8,16},{16,24},{1,9},{9,17},{17,25},{2,10},{10,18},{18,26},{... | collective-permute-start | bytes 1572872 | tf_op jit(solution)/shard_map/ppermute | solution.py:16
  372.8 3.8 collective-permute-start.21
  390.5 52.7 %copy-start.1 = (f32[2,2,4,512]{3,1,2,0:T(2,128)S(1)}, f32[2,2,4,512]{3,1,2,0:T(2,128)}, u32[]{:S(2)}) copy-start(f32[2,2,4,512]{3,1,2,0:T(2,128)} %copy-done) | copy-start | bytes 98308
  437.5 18.2 %all-to-all-start.1 = ((f32[2,4,32,512]{3,1,0,2:T(4,128)}), f32[2,4,32,512]{3,1,0,2:T(4,128)S(1)}, u32[]{:S(2)}, u32[]{:S(2)}) async-start(f32[2,4,32,512]{3,1,0,2:T(4,128)} %copy.63), calls=%async_computation.1 | async-start | bytes 1048576 | tf_op jit(solution)/shard_map/all_to_all | solution.py:117
